TPU v7x, 32 devices: a whole 2x2x4 slice. The times are simulated.
32 devices in a mesh: user: 8 (over z, y), item: 4 (over x, core).
Axes of the slice: x: 2, y: 2, z: 4, core: 2. Of those that a mesh axis runs over, the one named last changes fastest.
Arguments:
- theta_shape: float32 [16384, 1024], P('user', 'item'), may hold values from 0.3 to 3
- theta_rate: float32 [16384, 1024], P('user', 'item'), may hold values from 100 to 1000
- xi_rate: float32 [16384], P('user'), may hold values from 1 to 10
- beta_shape: float32 [4096, 1024], P('item', 'user'), may hold values from 0.3 to 3
- beta_rate: float32 [4096, 1024], P('item', 'user'), may hold values from 50 to 500
- eta_rate: float32 [4096], P('item'), may hold values from 1 to 10
- tile_slots: int32 [8, 4, 32], P('user', 'item'), may hold values from 0 to 31, as said below
- tile_counts: bfloat16 [8, 4, 32, 256, 256], P('user', 'item'), may hold values from 0 to 5, as said below
- live_tiles: int32 [8, 4], P('user', 'item'), may hold values from 1 to 32, as said below
Outputs:
- theta_shape_new: float32 [16384, 1024], P('user', 'item')
- theta_log_rate: float32 [16384, 1024], P('user', 'item')
- xi_rate_new: float32 [16384], P('user')
- beta_shape_new: float32 [4096, 1024], P('item', 'user')
- beta_log_rate: float32 [4096, 1024], P('item', 'user')
- eta_rate_new: float32 [4096], P('item')
Inputs may be any that keep to these rules, and one draw needn't show every extreme that they name: `tile_slots`: within one device's 32 slots the positions are distinct. `tile_counts`: whole numbers. `live_tiles`: some device uses all 32 slots.
All inputs are finite; a program needn't handle non-finite values.
Results may differ from a plain program's by a relative error of at most 0.0029.
Values may be sent and summed in bfloat16 or wider, within the bound.
No kernel may reach another device: no remote copies, remote signals or barrier semaphores. Data moves between devices by JAX's collectives and lax.ppermute only.
A program may use at most 128 MiB of HBM per device.

v0:
```python
import math
import jax
import jax.numpy as jnp
from jax import lax
from jax.sharding import PartitionSpec as P

BLK = 256
UB = 8
IB = 4
TMAX = 32
prior_a = 0.3
prior_a2 = 0.3
prior_b2 = 1.0
prior_c = 0.3
prior_c2 = 0.3
prior_d2 = 1.0


def exp_mean_log(shape_param, rate_param):
    return jnp.exp(lax.digamma(shape_param) - jnp.log(rate_param)).astype(jnp.bfloat16)


def on_device(
    theta_shape,
    theta_rate,
    xi_rate,
    beta_shape,
    beta_rate,
    eta_rate,
    tile_slots,
    tile_counts,
    live_tiles,
):
    user_width = lax.axis_size("user")
    item_width = lax.axis_size("item")
    user_index = lax.axis_index("user")
    item_index = lax.axis_index("item")
    theta_part = exp_mean_log(theta_shape, theta_rate)
    beta_part = exp_mean_log(beta_shape, beta_rate)
    theta_full = lax.all_gather(theta_part, "item", axis=1, tiled=True)
    beta_full = lax.all_gather(beta_part, "user", axis=1, tiled=True)
    factors = theta_full.shape[1]
    user_rows = theta_full.shape[0]
    item_rows = beta_full.shape[0]
    theta_blocks = theta_full.reshape(UB, BLK, factors)
    beta_blocks = beta_full.reshape(IB, BLK, factors)
    slot_list = tile_slots.reshape(TMAX)
    count_tiles = tile_counts.reshape(TMAX, BLK, BLK)
    used_slots = live_tiles.reshape(())
    user_blocks = slot_list // IB
    item_blocks = slot_list % IB
    group_size = math.gcd(TMAX, 8)

    def group_step(group_index, carried):
        user_acc, item_acc = carried
        first_slot = group_index * group_size
        rows_user = lax.dynamic_slice_in_dim(user_blocks, first_slot, group_size, 0)
        rows_item = lax.dynamic_slice_in_dim(item_blocks, first_slot, group_size, 0)
        counts = lax.dynamic_slice_in_dim(count_tiles, first_slot, group_size, 0).astype(
            jnp.float32
        )
        slot_mask = (first_slot + jnp.arange(group_size) < used_slots).astype(jnp.float32)
        counts = counts * slot_mask[:, None, None]
        users = jnp.take(theta_blocks, rows_user, axis=0)
        items = jnp.take(beta_blocks, rows_item, axis=0)
        denominator = jnp.einsum("tuk,tik->tui", users, items, preferred_element_type=jnp.float32)
        ratio_tile = (counts / denominator).astype(jnp.bfloat16)
        user_terms = jnp.einsum(
            "tui,tik->tuk", ratio_tile, items, preferred_element_type=jnp.float32
        )
        item_terms = jnp.einsum(
            "tui,tuk->tik", ratio_tile, users, preferred_element_type=jnp.float32
        )
        user_acc = user_acc.at[rows_user].add(user_terms)
        item_acc = item_acc.at[rows_item].add(item_terms)
        return (user_acc, item_acc)

    start_acc = (
        jnp.zeros((UB, BLK, factors), jnp.float32),
        jnp.zeros((IB, BLK, factors), jnp.float32),
    )
    group_count = TMAX // group_size
    user_acc, item_acc = lax.fori_loop(0, group_count, group_step, start_acc)
    user_acc = user_acc.reshape(user_rows, factors)
    item_acc = item_acc.reshape(item_rows, factors)
    beta_columns = factors // user_width
    theta_columns = factors // item_width
    beta_local = jnp.sum(beta_shape / beta_rate, axis=0)
    theta_local = jnp.sum(theta_shape / theta_rate, axis=0)
    beta_placed = lax.dynamic_update_slice_in_dim(
        jnp.zeros((factors,), jnp.float32), beta_local, user_index * beta_columns, 0
    )
    theta_placed = lax.dynamic_update_slice_in_dim(
        jnp.zeros((factors,), jnp.float32), theta_local, item_index * theta_columns, 0
    )
    beta_total, theta_total = lax.psum((beta_placed, theta_placed), ("user", "item"))
    xi_mean = (prior_a2 + factors * prior_a) / xi_rate
    user_summed = lax.psum(user_acc, "item")
    shape_whole = prior_a + theta_full.astype(jnp.float32) * user_summed
    rate_whole = xi_mean[:, None] + beta_total[None, :]
    xi_rate_new = prior_a2 / prior_b2 + jnp.sum(shape_whole / rate_whole, axis=1)
    theta_shape_new = lax.dynamic_slice_in_dim(
        shape_whole, item_index * theta_columns, theta_columns, 1
    )
    theta_rate_new = lax.dynamic_slice_in_dim(
        rate_whole, item_index * theta_columns, theta_columns, 1
    )
    item_share = lax.psum_scatter(item_acc, "user", scatter_dimension=1, tiled=True)
    beta_shape_new = prior_c + beta_part.astype(jnp.float32) * item_share
    eta_mean = (prior_c2 + factors * prior_c) / eta_rate
    theta_slice = lax.dynamic_slice_in_dim(theta_total, user_index * beta_columns, beta_columns, 0)
    beta_rate_new = eta_mean[:, None] + theta_slice[None, :]
    item_part = jnp.sum(beta_shape_new / beta_rate_new, axis=1)
    eta_rate_new = prior_c2 / prior_d2 + lax.psum(item_part, "user")
    return (
        theta_shape_new,
        jnp.log(theta_rate_new),
        xi_rate_new,
        beta_shape_new,
        jnp.log(beta_rate_new),
        eta_rate_new,
    )


def solution(mesh):
    in_specs = (
        P("user", "item"),
        P("user", "item"),
        P("user"),
        P("item", "user"),
        P("item", "user"),
        P("item"),
        P("user", "item", None),
        P("user", "item", None, None, None),
        P("user", "item"),
    )
    out_specs = (
        P("user", "item"),
        P("user", "item"),
        P("user"),
        P("item", "user"),
        P("item", "user"),
        P("item"),
    )
    return jax.shard_map(
        on_device, mesh=mesh, in_specs=in_specs, out_specs=out_specs, check_vma=False
    )
```

profile of v0, /device:TPU:0, one launch (start us, length us, event | category | flops | bytes accessed | tf_op | source)
XLA Modules:
  0.0 632.4 jit_solution(3128361467981943288)
XLA Ops:
  7.2 6.0 fusion.22
  13.3 17.6 %fusion.16 = (bf16[2048,256]{1,0:T(8,128)(2,1)}, f32[256]{0:T(256)}) fusion(f32[2048,256]{1,0:T(8,128)} %param.12, f32[2048,256]{1,0:T(8,128)} %param.11), kind=kLoop, calls=%fused_computation.36 | loop fusion | flops 41418496 | bytes 5243904 | tf_op jit(solution)/shard_map/convert_element_type | solution.py:20
  30.9 35.5 %all-gather.5.cloned.1.call-done = bf16[1024,1024]{1,0:T(8,128)(2,1)} async-done(((bf16[1024,128]{1,0:T(8,128)(2,1)}), bf16[1024,1024]{1,0:T(8,128)(2,1)}) %all-gather.5.cloned.1.call-update) | async-done | bytes 2097168 | tf_op jit(solution)/shard_map/all_gather | solution.py:41
  66.4 35.3 %all-gather.3.cloned.1.call-done = bf16[2048,1024]{1,0:T(8,128)(2,1)} async-done(((bf16[2048,256]{1,0:T(8,128)(2,1)}), bf16[2048,1024]{1,0:T(8,128)(2,1)}) %all-gather.3.cloned.1.call-update) | async-done | bytes 4194320 | tf_op jit(solution)/shard_map/all_gather | solution.py:40
  101.7 4.3 broadcast_in_dim.57
  106.0 2.5 broadcast_in_dim.58
  108.5 246.7 %while.15 = (s32[]{:T(128)}, f32[8,256,1024]{2,1,0:T(8,128)}, f32[4,256,1024]{2,1,0:T(8,128)}, s32[32]{0:T(128)S(1)}, bf16[32,256,256]{2,1,0:T(8,128)(2,1)}, /*i...) while((s32[]{:T(128)}, f32[8,256,1024]{2,1,0:T(8,128)}, ...), condition=%wide.region_3.4_spmd, body=%wide.region_0.3_spmd.sunk | while | flops 3238004736 | bytes 134226640 | solution.py:83
  108.6 5.0 gather_fusion
  113.6 2.8 gather_fusion.1
  116.4 5.0 fusion.28
  121.4 0.7 compare_convert_fusion.2
  122.1 6.0 fusion.30
  128.1 17.1 %scatter_fusion.1 = f32[4,256,1024]{2,1,0:T(8,128)} fusion(f32[4,256,1024]{2,1,0:T(8,128)} %get-tuple-element.281, s32[8]{0:T(128)S(1)} %get-tuple-element.264, f32[8,256,1024]{2,1,0:T(8,128)} %fusion.30), kind=kCustom, calls=%fused_computation.3.clone.1 | custom fusion | flops 2097152 | bytes 25165856 | tf_op jit(solution)/shard_map/while/body/eval_jaxpr/scatter-add | solution.py:75
  145.2 7.7 %fusion.29 = f32[8,256,1024]{2,1,0:T(8,128)} fusion(f32[8,256,256]{2,1,0:T(8,128)} %copy-done.8, bf16[8,256,1024]{2,1,0:T(8,128)(2,1)} %gather_fusion.1, pred[8]{0:T(512)(128)(4,1)S(1)} %get-tuple-element.265, f32[8]{0:T(128)S(1)} %compare_convert_fusion.2, bf16[32,256,256]{2,1,0:T(8,128)(2,1)} %get-tuple-element.296, s32[]{:T(128)S(6)} %select_n.90), kind=kOutput, calls=%fused_computation.8.clone.1 | convolution fusion | flops 1077936128 | bytes 15728684 | tf_op jit(solution)/shard_map/while/body/eval_jaxpr/tui,tik->tuk/dot_general | solution.py:68
  152.9 17.4 %scatter_fusion = f32[8,256,1024]{2,1,0:T(8,128)} fusion(f32[8,256,1024]{2,1,0:T(8,128)} %get-tuple-element.280, s32[8]{0:T(128)S(1)} %get-tuple-element.262, f32[8,256,1024]{2,1,0:T(8,128)} %fusion.29), kind=kCustom, calls=%fused_computation.2.clone.1 | custom fusion | flops 2097152 | bytes 25165856 | tf_op jit(solution)/shard_map/while/body/eval_jaxpr/scatter-add | solution.py:74
  170.4 5.0 gather_fusion
  175.4 2.8 gather_fusion.1
  178.2 5.0 fusion.28
  183.2 0.7 compare_convert_fusion.2
  183.9 6.0 fusion.30
  189.9 17.1 %scatter_fusion.1 = f32[4,256,1024]{2,1,0:T(8,128)} fusion(f32[4,256,1024]{2,1,0:T(8,128)} %get-tuple-element.281, s32[8]{0:T(128)S(1)} %get-tuple-element.264, f32[8,256,1024]{2,1,0:T(8,128)} %fusion.30), kind=kCustom, calls=%fused_computation.3.clone.1 | custom fusion | flops 2097152 | bytes 25165856 | tf_op jit(solution)/shard_map/while/body/eval_jaxpr/scatter-add | solution.py:75
  207.0 7.7 %fusion.29 = f32[8,256,1024]{2,1,0:T(8,128)} fusion(f32[8,256,256]{2,1,0:T(8,128)} %copy-done.8, bf16[8,256,1024]{2,1,0:T(8,128)(2,1)} %gather_fusion.1, pred[8]{0:T(512)(128)(4,1)S(1)} %get-tuple-element.265, f32[8]{0:T(128)S(1)} %compare_convert_fusion.2, bf16[32,256,256]{2,1,0:T(8,128)(2,1)} %get-tuple-element.296, s32[]{:T(128)S(6)} %select_n.90), kind=kOutput, calls=%fused_computation.8.clone.1 | convolution fusion | flops 1077936128 | bytes 15728684 | tf_op jit(solution)/shard_map/while/body/eval_jaxpr/tui,tik->tuk/dot_general | solution.py:68
  214.7 17.5 %scatter_fusion = f32[8,256,1024]{2,1,0:T(8,128)} fusion(f32[8,256,1024]{2,1,0:T(8,128)} %get-tuple-element.280, s32[8]{0:T(128)S(1)} %get-tuple-element.262, f32[8,256,1024]{2,1,0:T(8,128)} %fusion.29), kind=kCustom, calls=%fused_computation.2.clone.1 | custom fusion | flops 2097152 | bytes 25165856 | tf_op jit(solution)/shard_map/while/body/eval_jaxpr/scatter-add | solution.py:74
  232.2 5.0 gather_fusion
  237.2 2.8 gather_fusion.1
  240.0 5.0 fusion.28
  245.1 0.7 compare_convert_fusion.2
  245.8 6.0 fusion.30
  251.7 17.0 %scatter_fusion.1 = f32[4,256,1024]{2,1,0:T(8,128)} fusion(f32[4,256,1024]{2,1,0:T(8,128)} %get-tuple-element.281, s32[8]{0:T(128)S(1)} %get-tuple-element.264, f32[8,256,1024]{2,1,0:T(8,128)} %fusion.30), kind=kCustom, calls=%fused_computation.3.clone.1 | custom fusion | flops 2097152 | bytes 25165856 | tf_op jit(solution)/shard_map/while/body/eval_jaxpr/scatter-add | solution.py:75
  268.7 7.7 %fusion.29 = f32[8,256,1024]{2,1,0:T(8,128)} fusion(f32[8,256,256]{2,1,0:T(8,128)} %copy-done.8, bf16[8,256,1024]{2,1,0:T(8,128)(2,1)} %gather_fusion.1, pred[8]{0:T(512)(128)(4,1)S(1)} %get-tuple-element.265, f32[8]{0:T(128)S(1)} %compare_convert_fusion.2, bf16[32,256,256]{2,1,0:T(8,128)(2,1)} %get-tuple-element.296, s32[]{:T(128)S(6)} %select_n.90), kind=kOutput, calls=%fused_computation.8.clone.1 | convolution fusion | flops 1077936128 | bytes 15728684 | tf_op jit(solution)/shard_map/while/body/eval_jaxpr/tui,tik->tuk/dot_general | solution.py:68
  276.4 17.3 %scatter_fusion = f32[8,256,1024]{2,1,0:T(8,128)} fusion(f32[8,256,1024]{2,1,0:T(8,128)} %get-tuple-element.280, s32[8]{0:T(128)S(1)} %get-tuple-element.262, f32[8,256,1024]{2,1,0:T(8,128)} %fusion.29), kind=kCustom, calls=%fused_computation.2.clone.1 | custom fusion | flops 2097152 | bytes 25165856 | tf_op jit(solution)/shard_map/while/body/eval_jaxpr/scatter-add | solution.py:74
  293.8 5.0 gather_fusion
  298.8 2.8 gather_fusion.1
  301.6 5.0 fusion.28
  306.7 0.7 compare_convert_fusion.2
  307.4 6.0 fusion.30
  313.3 17.3 %scatter_fusion.1 = f32[4,256,1024]{2,1,0:T(8,128)} fusion(f32[4,256,1024]{2,1,0:T(8,128)} %get-tuple-element.281, s32[8]{0:T(128)S(1)} %get-tuple-element.264, f32[8,256,1024]{2,1,0:T(8,128)} %fusion.30), kind=kCustom, calls=%fused_computation.3.clone.1 | custom fusion | flops 2097152 | bytes 25165856 | tf_op jit(solution)/shard_map/while/body/eval_jaxpr/scatter-add | solution.py:75
  330.7 7.7 %fusion.29 = f32[8,256,1024]{2,1,0:T(8,128)} fusion(f32[8,256,256]{2,1,0:T(8,128)} %copy-done.8, bf16[8,256,1024]{2,1,0:T(8,128)(2,1)} %gather_fusion.1, pred[8]{0:T(512)(128)(4,1)S(1)} %get-tuple-element.265, f32[8]{0:T(128)S(1)} %compare_convert_fusion.2, bf16[32,256,256]{2,1,0:T(8,128)(2,1)} %get-tuple-element.296, s32[]{:T(128)S(6)} %select_n.90), kind=kOutput, calls=%fused_computation.8.clone.1 | convolution fusion | flops 1077936128 | bytes 15728684 | tf_op jit(solution)/shard_map/while/body/eval_jaxpr/tui,tik->tuk/dot_general | solution.py:68
  338.4 16.8 %scatter_fusion = f32[8,256,1024]{2,1,0:T(8,128)} fusion(f32[8,256,1024]{2,1,0:T(8,128)} %get-tuple-element.280, s32[8]{0:T(128)S(1)} %get-tuple-element.262, f32[8,256,1024]{2,1,0:T(8,128)} %fusion.29), kind=kCustom, calls=%fused_computation.2.clone.1 | custom fusion | flops 2097152 | bytes 25165856 | tf_op jit(solution)/shard_map/while/body/eval_jaxpr/scatter-add | solution.py:74
  356.3 41.7 %all-reduce = (f32[1024]{0:T(1024)S(1)}, f32[1024]{0:T(1024)S(1)}) all-reduce(f32[1024]{0:T(1024)S(1)} %dynamic_update_slice.6, f32[1024]{0:T(1024)S(1)} %dynamic_update_slice.7), channel_id=1, replica_groups=mesh['user'=8,'item'=4] {'user','item'}, use_global_device_ids=true, to_apply=%region_6.7 | all-reduce | flops 2048 | bytes 16384 | tf_op jit(solution)/shard_map/psum | solution.py:96
  398.1 112.6 %all-reduce.3.cloned.1.call-done = f32[2048,1024]{1,0:T(8,128)} async-done(((f32[2048,1024]{1,0:T(8,128)}), f32[2048,1024]{1,0:T(8,128)}) %all-reduce.3.cloned.1.call-update) | async-done | bytes 8388624 | tf_op jit(solution)/shard_map/psum | solution.py:98
  510.7 6.0 divide_reduce_fusion
  516.7 0.6 broadcast_add_fusion.1
  517.3 2.5 dynamic-slice_log_fusion
  519.8 83.2 %reduce-scatter.2.cloned.1.call-done = f32[1024,128]{1,0:T(8,128)} async-done(((f32[1024,1024]{1,0:T(8,128)}), f32[1024,128]{1,0:T(8,128)}) %reduce-scatter.2.cloned.1.call-update) | async-done | bytes 524304 | tf_op jit(solution)/shard_map/reduce_scatter | solution.py:108
  603.0 2.2 fusion.23
  605.2 20.1 %psum.31 = f32[1024]{0:T(1024)S(1)} all-reduce(f32[1024]{0:T(1024)S(1)} %get-tuple-element.187), channel_id=1, replica_groups=mesh['user'=8,'item'=4] {'user'}, use_global_device_ids=true, to_apply=%region_12.13 | all-reduce | flops 1024 | bytes 8192 | tf_op jit(solution)/shard_map/psum | solution.py:114
  625.3 0.6 broadcast_add_fusion.2
  (58 shorter events, 1.8 us)
Async XLA Ops:
  7.2 59.2 %all-gather.5.cloned.1.call-start = ((), (), s32[]{:S(2)}) async-start(), calls=%async_computation.2 | async-start | bytes 2359296 | tf_op jit(solution)/shard_map/all_gather | solution.py:41
  13.2 17.7 %copy-start.7 = (s32[1,1,32]{2,1,0:T(1,128)S(1)}, s32[1,1,32]{2,1,0:T(1,128)}, u32[]{:S(2)}) copy-start(s32[1,1,32]{2,1,0:T(1,128)} %param.17) | copy-start | bytes 388
  13.2 88.5 %all-gather.3.cloned.1.call-start = ((), (), s32[]{:S(2)}) async-start(), calls=%async_computation.1 | async-start | bytes 5242880 | tf_op jit(solution)/shard_map/all_gather | solution.py:40
  30.9 479.8 %all-reduce.3.cloned.1.call-start = ((), (), s32[]{:S(2)}) async-start(), calls=%async_computation.3 | async-start | bytes 16777216 | tf_op jit(solution)/shard_map/psum | solution.py:98
  106.0 2.5 copy-start
  116.4 5.8 copy-start.1
  121.4 6.7 %copy-start.8 = (f32[8,256,256]{2,1,0:T(8,128)}, f32[8,256,256]{2,1,0:T(8,128)S(1)}, u32[]{:S(2)}) copy-start(f32[8,256,256]{2,1,0:T(8,128)S(1)} %fusion.28) | copy-start | bytes 6291460 | tf_op jit(solution)/shard_map/while
  178.1 5.8 copy-start.1
  183.2 6.7 %copy-start.8 = (f32[8,256,256]{2,1,0:T(8,128)}, f32[8,256,256]{2,1,0:T(8,128)S(1)}, u32[]{:S(2)}) copy-start(f32[8,256,256]{2,1,0:T(8,128)S(1)} %fusion.28) | copy-start | bytes 6291460 | tf_op jit(solution)/shard_map/while
  240.0 5.8 copy-start.1
  245.1 6.7 %copy-start.8 = (f32[8,256,256]{2,1,0:T(8,128)}, f32[8,256,256]{2,1,0:T(8,128)S(1)}, u32[]{:S(2)}) copy-start(f32[8,256,256]{2,1,0:T(8,128)S(1)} %fusion.28) | copy-start | bytes 6291460 | tf_op jit(solution)/shard_map/while
  301.6 5.8 copy-start.1
  306.7 6.7 %copy-start.8 = (f32[8,256,256]{2,1,0:T(8,128)}, f32[8,256,256]{2,1,0:T(8,128)S(1)}, u32[]{:S(2)}) copy-start(f32[8,256,256]{2,1,0:T(8,128)S(1)} %fusion.28) | copy-start | bytes 6291460 | tf_op jit(solution)/shard_map/while
  355.2 247.8 %reduce-scatter.2.cloned.1.call-start = ((), (), s32[]{:S(2)}) async-start(), calls=%async_computation.4 | async-start | bytes 4718592 | tf_op jit(solution)/shard_map/reduce_scatter | solution.py:108
  355.2 0.7 copy-start.5
  355.3 0.8 copy-start.6
  355.3 42.8 %copy-start.4 = (f32[1024]{0:T(1024)S(1)}, f32[1024]{0:T(1024)}, u32[]{:S(2)}) copy-start(f32[1024]{0:T(1024)} %param.16) | copy-start | bytes 12292
  355.3 42.8 %copy-start.3 = (f32[2048]{0:T(1024)S(1)}, f32[2048]{0:T(1024)}, u32[]{:S(2)}) copy-start(f32[2048]{0:T(1024)} %param.13) | copy-start | bytes 24580
  517.3 85.7 %copy-start.2 = (bf16[1024,128]{1,0:T(8,128)(2,1)S(1)}, bf16[1024,128]{1,0:T(8,128)(2,1)}, u32[]{:S(2)}) copy-start(bf16[1024,128]{1,0:T(8,128)(2,1)} %get-tuple-element.195) | copy-start | bytes 786436
Sparse Core Ops, SparseCore 0:
  13.3 53.0 all-gather.4
  68.5 33.1 all-gather.2
  355.3 155.3 all-reduce.2
  514.2 88.8 reduce-scatter.1
where the time goes:
time: 633 us; the launch traced here: 632 us
  waiting for transfers between devices  267 us (42%)
  other arithmetic  173 us (27%)
  matrix products  74.9 us (12%)
  blocking collectives  61.8 us (10%)
  local copies, waits for them, and re-layouts  41 us (6%)
  between operations  13.9 us (2%)
    psum x1, waiting for transfers between devices, on_device(): user_summed = lax.psum(user_acc, 'item')  113 us
    reduce_scatter x1, waiting for transfers between devices, on_device(): lax.psum_scatter(item_acc, 'user', scatter_dimension=1, tiled=True)  83.2 us
    scatter-add x4, other arithmetic, group_step(): user_acc = user_acc.at[rows_user].add(user_terms)  69 us
    scatter-add x4, other arithmetic, group_step(): item_acc = item_acc.at[rows_item].add(item_terms)  68.5 us
    psum x1, blocking collectives, on_device(): lax.psum((beta_placed, theta_placed), ('user', 'item'))  41.7 us
    all_gather x1, waiting for transfers between devices, on_device(): beta_full = lax.all_gather(beta_part, 'user', axis=1, tiled=True)  35.5 us
    all_gather x1, waiting for transfers between devices, on_device(): theta_full = lax.all_gather(theta_part, 'item', axis=1, tiled=True)  35.3 us
    dot_general x4, matrix products, group_step(): jnp.einsum('tui,tik->tuk', ratio_tile, items, preferred_element_type=jnp....  30.8 us
  transfers between devices with their start and end apart: 4, of which 4 were waited for; matrix products, arithmetic and copies ran while one was open for 4% of the time, Pallas kernels for 0%

commit v1 on v0

--- a/solution.py
+++ b/solution.py
@@ -14,6 +14,31 @@
 prior_c = 0.3
 prior_c2 = 0.3
 prior_d2 = 1.0
+
+
+def name_sheet(v0):
+    p_next = lax.axis_size("user")
+    y_new = lax.axis_index("user")
+    tall, next_value, before = (p_next, y_new, v0.shape[1])
+    history = tuple((rr * tall if s == 1 else rr for s, rr in enumerate(v0.shape)))
+    field_out = jnp.zeros(history, v0.dtype)
+    m_next = lax.dynamic_update_slice_in_dim(field_out, v0, next_value * before, axis=1)
+    b_now = wide_out = v0
+    j = 1
+    while j < tall // 2 + 1:
+        inter = tuple(((s, (s + 1) % tall) for s in range(tall)))
+        b_now = lax.ppermute(b_now, "user", inter)
+        m_next = lax.dynamic_update_slice_in_dim(
+            m_next, b_now, (next_value - j) % tall * before, axis=1
+        )
+        if 2 * j < tall:
+            state_next = tuple(((s, (s - 1) % tall) for s in range(tall)))
+            wide_out = lax.ppermute(wide_out, "user", state_next)
+            m_next = lax.dynamic_update_slice_in_dim(
+                m_next, wide_out, (next_value + j) % tall * before, axis=1
+            )
+        j += 1
+    return m_next
 
 
 def exp_mean_log(shape_param, rate_param):
@@ -38,7 +63,7 @@
     theta_part = exp_mean_log(theta_shape, theta_rate)
     beta_part = exp_mean_log(beta_shape, beta_rate)
     theta_full = lax.all_gather(theta_part, "item", axis=1, tiled=True)
-    beta_full = lax.all_gather(beta_part, "user", axis=1, tiled=True)
+    beta_full = name_sheet(beta_part)
     factors = theta_full.shape[1]
     user_rows = theta_full.shape[0]
     item_rows = beta_full.shape[0]

time: 633 us -> 611 us (0.965)
  waiting for transfers between devices: 267 us -> 227 us
  starting transfers between devices: 0.16 us -> 20.4 us
    all_gather x1 -> x0, waiting for transfers between devices: 35.5 us -> none  [on_device(): beta_full = lax.all_gather(beta_part, 'user', axis=1, tiled=True)]
    all_gather x1, waiting for transfers between devices: 35.3 us -> 0.02 us  [on_device(): theta_full = lax.all_gather(theta_part, 'item', axis=1, tiled=True)]
    ppermute x0 -> x7, waiting for transfers between devices: none -> 30.7 us  [the longest x4 30.7 us: name_sheet(): b_now = lax.ppermute(b_now, 'user', inter)]
    ppermute x0 -> x7, starting transfers between devices: none -> 20.3 us  [the longest x4 10.5 us: name_sheet(): b_now = lax.ppermute(b_now, 'user', inter)]
    convert_element_type x2 -> x1, other arithmetic: 23.5 us -> 17.6 us  [exp_mean_log(): jnp.exp(lax.digamma(shape_param) - jnp.log(rate_param)).astype(jnp.bfloat16)]
  transfers between devices with their start and end apart: 4 -> 10, of which waited for: 4 -> 6; matrix products, arithmetic and copies ran while one was open for 4% -> 2% of each run, Pallas kernels for 0% -> 0%
where the time goes in v1:
time: 611 us; the launch traced here: 610 us
  waiting for transfers between devices  227 us (37%)
  other arithmetic  171 us (28%)
  matrix products  75.1 us (12%)
  blocking collectives  58.9 us (10%)
  local copies, waits for them, and re-layouts  43.1 us (7%)
  starting transfers between devices  20.4 us (3%)
  between operations  14.1 us (2%)
    psum x1, waiting for transfers between devices, on_device(): user_summed = lax.psum(user_acc, 'item')  113 us
    reduce_scatter x1, waiting for transfers between devices, on_device(): lax.psum_scatter(item_acc, 'user', scatter_dimension=1, tiled=True)  83.4 us
    scatter-add x4, other arithmetic, group_step(): user_acc = user_acc.at[rows_user].add(user_terms)  69 us
    scatter-add x4, other arithmetic, group_step(): item_acc = item_acc.at[rows_item].add(item_terms)  68.1 us
    psum x1, blocking collectives, on_device(): lax.psum((beta_placed, theta_placed), ('user', 'item'))  38.8 us
    dot_general x4, matrix products, group_step(): jnp.einsum('tui,tik->tuk', ratio_tile, items, preferred_element_type=jnp....  30.9 us
    ppermute x4, waiting for transfers between devices, name_sheet(): b_now = lax.ppermute(b_now, 'user', inter)  30.7 us
    dot_general x4, matrix products, group_step(): jnp.einsum('tui,tuk->tik', ratio_tile, users, preferred_element_type=jnp....  24 us
  transfers between devices with their start and end apart: 10, of which 6 were waited for; matrix products, arithmetic and copies ran while one was open for 2% of the time, Pallas kernels for 0%

profile of v1, /device:TPU:0, one launch (start us, length us, event | category | flops | bytes accessed | tf_op | source)
XLA Modules:
  0.0 610.1 jit_solution(15432598891383006339)
XLA Ops:
  7.2 17.6 %fusion.16 = (bf16[2048,256]{1,0:T(8,128)(2,1)}, f32[256]{0:T(256)}) fusion(f32[2048,256]{1,0:T(8,128)} %param.12, f32[2048,256]{1,0:T(8,128)} %param.11), kind=kLoop, calls=%fused_computation.36 | loop fusion | flops 41418496 | bytes 5243904 | tf_op jit(solution)/shard_map/convert_element_type | solution.py:45
  26.0 3.8 constant_dynamic-update-slice_fusion.7
  29.8 3.0 collective-permute-start
  32.9 3.7 collective-permute-start.1
  36.5 7.5 %collective-permute-done = bf16[1024,128]{1,0:T(8,128)(2,1)S(1)} collective-permute-done((bf16[1024,128]{1,0:T(8,128)(2,1)S(1)}, bf16[1024,128]{1,0:T(8,128)(2,1)S(1)}, u32[]{:S(2)}, u32[]{:S(2)}) %collective-permute-start) | collective-permute-done | bytes 262176 | tf_op jit(solution)/shard_map/ppermute | solution.py:30
  44.0 2.5 collective-permute-start.2
  46.5 3.0 collective-permute-start.3
  49.7 7.2 %collective-permute-done.2 = bf16[1024,128]{1,0:T(8,128)(2,1)S(1)} collective-permute-done((bf16[1024,128]{1,0:T(8,128)(2,1)S(1)}, bf16[1024,128]{1,0:T(8,128)(2,1)S(1)}, u32[]{:S(2)}, u32[]{:S(2)}) %collective-permute-start.2) | collective-permute-done | bytes 262176 | tf_op jit(solution)/shard_map/ppermute | solution.py:30
  59.6 3.1 collective-permute-start.5
  62.8 6.4 %collective-permute-done.4 = bf16[1024,128]{1,0:T(8,128)(2,1)S(1)} collective-permute-done((bf16[1024,128]{1,0:T(8,128)(2,1)S(1)}, bf16[1024,128]{1,0:T(8,128)(2,1)S(1)}, u32[]{:S(2)}, u32[]{:S(2)}) %collective-permute-start.4) | collective-permute-done | bytes 262176 | tf_op jit(solution)/shard_map/ppermute | solution.py:30
  72.0 9.6 %collective-permute-done.6 = bf16[1024,128]{1,0:T(8,128)(2,1)S(1)} collective-permute-done((bf16[1024,128]{1,0:T(8,128)(2,1)S(1)}, bf16[1024,128]{1,0:T(8,128)(2,1)S(1)}, u32[]{:S(2)}, u32[]{:S(2)}) %collective-permute-start.6) | collective-permute-done | bytes 262176 | tf_op jit(solution)/shard_map/ppermute | solution.py:30
  81.7 4.3 broadcast_in_dim.60
  86.0 2.5 broadcast_in_dim.61
  88.4 246.4 %while.15 = (s32[]{:T(128)}, f32[8,256,1024]{2,1,0:T(8,128)}, f32[4,256,1024]{2,1,0:T(8,128)}, s32[32]{0:T(128)S(1)}, bf16[32,256,256]{2,1,0:T(8,128)(2,1)}, /*i...) while((s32[]{:T(128)}, f32[8,256,1024]{2,1,0:T(8,128)}, ...), condition=%wide.region_3.4_spmd, body=%wide.region_0.3_spmd.sunk | while | flops 3238004736 | bytes 134226640 | solution.py:108
  88.5 4.9 gather_fusion
  93.5 2.8 gather_fusion.1
  96.3 5.0 fusion.29
  102.0 6.0 fusion.31
  108.0 16.8 %scatter_fusion.1 = f32[4,256,1024]{2,1,0:T(8,128)} fusion(f32[4,256,1024]{2,1,0:T(8,128)} %get-tuple-element.281, s32[8]{0:T(128)S(1)} %get-tuple-element.264, f32[8,256,1024]{2,1,0:T(8,128)} %fusion.31), kind=kCustom, calls=%fused_computation.3.clone.1 | custom fusion | flops 2097152 | bytes 25165856 | tf_op jit(solution)/shard_map/while/body/eval_jaxpr/scatter-add | solution.py:100
  124.8 7.7 %fusion.30 = f32[8,256,1024]{2,1,0:T(8,128)} fusion(f32[8,256,256]{2,1,0:T(8,128)} %copy-done.11, bf16[8,256,1024]{2,1,0:T(8,128)(2,1)} %gather_fusion.1, pred[8]{0:T(512)(128)(4,1)S(1)} %get-tuple-element.265, f32[8]{0:T(128)S(1)} %compare_convert_fusion.2, bf16[32,256,256]{2,1,0:T(8,128)(2,1)} %get-tuple-element.296, s32[]{:T(128)S(6)} %select_n.156), kind=kOutput, calls=%fused_computation.8.clone.1 | convolution fusion | flops 1077936128 | bytes 15728684 | tf_op jit(solution)/shard_map/while/body/eval_jaxpr/tui,tik->tuk/dot_general | solution.py:93
  132.5 17.4 %scatter_fusion = f32[8,256,1024]{2,1,0:T(8,128)} fusion(f32[8,256,1024]{2,1,0:T(8,128)} %get-tuple-element.280, s32[8]{0:T(128)S(1)} %get-tuple-element.262, f32[8,256,1024]{2,1,0:T(8,128)} %fusion.30), kind=kCustom, calls=%fused_computation.2.clone.1 | custom fusion | flops 2097152 | bytes 25165856 | tf_op jit(solution)/shard_map/while/body/eval_jaxpr/scatter-add | solution.py:99
  150.1 4.9 gather_fusion
  155.0 2.8 gather_fusion.1
  157.8 5.0 fusion.29
  163.6 6.0 fusion.31
  169.6 17.1 %scatter_fusion.1 = f32[4,256,1024]{2,1,0:T(8,128)} fusion(f32[4,256,1024]{2,1,0:T(8,128)} %get-tuple-element.281, s32[8]{0:T(128)S(1)} %get-tuple-element.264, f32[8,256,1024]{2,1,0:T(8,128)} %fusion.31), kind=kCustom, calls=%fused_computation.3.clone.1 | custom fusion | flops 2097152 | bytes 25165856 | tf_op jit(solution)/shard_map/while/body/eval_jaxpr/scatter-add | solution.py:100
  186.7 7.7 %fusion.30 = f32[8,256,1024]{2,1,0:T(8,128)} fusion(f32[8,256,256]{2,1,0:T(8,128)} %copy-done.11, bf16[8,256,1024]{2,1,0:T(8,128)(2,1)} %gather_fusion.1, pred[8]{0:T(512)(128)(4,1)S(1)} %get-tuple-element.265, f32[8]{0:T(128)S(1)} %compare_convert_fusion.2, bf16[32,256,256]{2,1,0:T(8,128)(2,1)} %get-tuple-element.296, s32[]{:T(128)S(6)} %select_n.156), kind=kOutput, calls=%fused_computation.8.clone.1 | convolution fusion | flops 1077936128 | bytes 15728684 | tf_op jit(solution)/shard_map/while/body/eval_jaxpr/tui,tik->tuk/dot_general | solution.py:93
  194.4 17.5 %scatter_fusion = f32[8,256,1024]{2,1,0:T(8,128)} fusion(f32[8,256,1024]{2,1,0:T(8,128)} %get-tuple-element.280, s32[8]{0:T(128)S(1)} %get-tuple-element.262, f32[8,256,1024]{2,1,0:T(8,128)} %fusion.30), kind=kCustom, calls=%fused_computation.2.clone.1 | custom fusion | flops 2097152 | bytes 25165856 | tf_op jit(solution)/shard_map/while/body/eval_jaxpr/scatter-add | solution.py:99
  212.0 4.9 gather_fusion
  216.9 2.8 gather_fusion.1
  219.7 5.0 fusion.29
  225.5 6.0 fusion.31
  231.5 16.9 %scatter_fusion.1 = f32[4,256,1024]{2,1,0:T(8,128)} fusion(f32[4,256,1024]{2,1,0:T(8,128)} %get-tuple-element.281, s32[8]{0:T(128)S(1)} %get-tuple-element.264, f32[8,256,1024]{2,1,0:T(8,128)} %fusion.31), kind=kCustom, calls=%fused_computation.3.clone.1 | custom fusion | flops 2097152 | bytes 25165856 | tf_op jit(solution)/shard_map/while/body/eval_jaxpr/scatter-add | solution.py:100
  248.4 7.7 %fusion.30 = f32[8,256,1024]{2,1,0:T(8,128)} fusion(f32[8,256,256]{2,1,0:T(8,128)} %copy-done.11, bf16[8,256,1024]{2,1,0:T(8,128)(2,1)} %gather_fusion.1, pred[8]{0:T(512)(128)(4,1)S(1)} %get-tuple-element.265, f32[8]{0:T(128)S(1)} %compare_convert_fusion.2, bf16[32,256,256]{2,1,0:T(8,128)(2,1)} %get-tuple-element.296, s32[]{:T(128)S(6)} %select_n.156), kind=kOutput, calls=%fused_computation.8.clone.1 | convolution fusion | flops 1077936128 | bytes 15728684 | tf_op jit(solution)/shard_map/while/body/eval_jaxpr/tui,tik->tuk/dot_general | solution.py:93
  256.1 17.4 %scatter_fusion = f32[8,256,1024]{2,1,0:T(8,128)} fusion(f32[8,256,1024]{2,1,0:T(8,128)} %get-tuple-element.280, s32[8]{0:T(128)S(1)} %get-tuple-element.262, f32[8,256,1024]{2,1,0:T(8,128)} %fusion.30), kind=kCustom, calls=%fused_computation.2.clone.1 | custom fusion | flops 2097152 | bytes 25165856 | tf_op jit(solution)/shard_map/while/body/eval_jaxpr/scatter-add | solution.py:99
  273.6 4.9 gather_fusion
  278.6 2.8 gather_fusion.1
  281.4 5.0 fusion.29
  287.1 6.0 fusion.31
  293.1 17.3 %scatter_fusion.1 = f32[4,256,1024]{2,1,0:T(8,128)} fusion(f32[4,256,1024]{2,1,0:T(8,128)} %get-tuple-element.281, s32[8]{0:T(128)S(1)} %get-tuple-element.264, f32[8,256,1024]{2,1,0:T(8,128)} %fusion.31), kind=kCustom, calls=%fused_computation.3.clone.1 | custom fusion | flops 2097152 | bytes 25165856 | tf_op jit(solution)/shard_map/while/body/eval_jaxpr/scatter-add | solution.py:100
  310.4 7.7 %fusion.30 = f32[8,256,1024]{2,1,0:T(8,128)} fusion(f32[8,256,256]{2,1,0:T(8,128)} %copy-done.11, bf16[8,256,1024]{2,1,0:T(8,128)(2,1)} %gather_fusion.1, pred[8]{0:T(512)(128)(4,1)S(1)} %get-tuple-element.265, f32[8]{0:T(128)S(1)} %compare_convert_fusion.2, bf16[32,256,256]{2,1,0:T(8,128)(2,1)} %get-tuple-element.296, s32[]{:T(128)S(6)} %select_n.156), kind=kOutput, calls=%fused_computation.8.clone.1 | convolution fusion | flops 1077936128 | bytes 15728684 | tf_op jit(solution)/shard_map/while/body/eval_jaxpr/tui,tik->tuk/dot_general | solution.py:93
  318.2 16.7 %scatter_fusion = f32[8,256,1024]{2,1,0:T(8,128)} fusion(f32[8,256,1024]{2,1,0:T(8,128)} %get-tuple-element.280, s32[8]{0:T(128)S(1)} %get-tuple-element.262, f32[8,256,1024]{2,1,0:T(8,128)} %fusion.30), kind=kCustom, calls=%fused_computation.2.clone.1 | custom fusion | flops 2097152 | bytes 25165856 | tf_op jit(solution)/shard_map/while/body/eval_jaxpr/scatter-add | solution.py:99
  336.7 38.8 %all-reduce = (f32[1024]{0:T(1024)S(1)}, f32[1024]{0:T(1024)S(1)}) all-reduce(f32[1024]{0:T(1024)S(1)} %dynamic_update_slice.38, f32[1024]{0:T(1024)S(1)} %dynamic_update_slice.39), channel_id=1, replica_groups=mesh['user'=8,'item'=4] {'user','item'}, use_global_device_ids=true, to_apply=%region_6.7 | all-reduce | flops 2048 | bytes 16384 | tf_op jit(solution)/shard_map/psum | solution.py:121
  375.7 112.6 %all-reduce.3.cloned.1.call-done = f32[2048,1024]{1,0:T(8,128)} async-done(((f32[2048,1024]{1,0:T(8,128)}), f32[2048,1024]{1,0:T(8,128)}) %all-reduce.3.cloned.1.call-update) | async-done | bytes 8388624 | tf_op jit(solution)/shard_map/psum | solution.py:123
  488.3 6.0 divide_reduce_fusion
  494.9 2.5 dynamic-slice_log_fusion
  497.4 83.4 %reduce-scatter.2.cloned.1.call-done = f32[1024,128]{1,0:T(8,128)} async-done(((f32[1024,1024]{1,0:T(8,128)}), f32[1024,128]{1,0:T(8,128)}) %reduce-scatter.2.cloned.1.call-update) | async-done | bytes 524304 | tf_op jit(solution)/shard_map/reduce_scatter | solution.py:133
  582.9 20.1 %psum.31 = f32[1024]{0:T(1024)S(1)} all-reduce(f32[1024]{0:T(1024)S(1)} %get-tuple-element.187), channel_id=1, replica_groups=mesh['user'=8,'item'=4] {'user'}, use_global_device_ids=true, to_apply=%region_12.13 | all-reduce | flops 1024 | bytes 8192 | tf_op jit(solution)/shard_map/psum | solution.py:139
  (84 shorter events, 15.2 us)
Async XLA Ops:
  7.2 74.5 %all-gather.2.cloned.1.call-start = ((), (), s32[]{:S(2)}) async-start(), calls=%async_computation.1 | async-start | bytes 5242880 | tf_op jit(solution)/shard_map/all_gather | solution.py:65
  24.8 1.0 copy-start.1
  24.8 1.2 copy-start.3
  24.8 24.7 %copy-start.10 = (s32[1,1,32]{2,1,0:T(1,128)S(1)}, s32[1,1,32]{2,1,0:T(1,128)}, u32[]{:S(2)}) copy-start(s32[1,1,32]{2,1,0:T(1,128)} %param.17) | copy-start | bytes 388
  24.8 463.4 %all-reduce.3.cloned.1.call-start = ((), (), s32[]{:S(2)}) async-start(), calls=%async_computation.2 | async-start | bytes 16777216 | tf_op jit(solution)/shard_map/psum | solution.py:123
  29.8 3.1 copy-start.5
  29.8 14.2 %collective-permute-start = (bf16[1024,128]{1,0:T(8,128)(2,1)S(1)}, bf16[1024,128]{1,0:T(8,128)(2,1)S(1)}, u32[]{:S(2)}, u32[]{:S(2)}) collective-permute-start(bf16[1024,128]{1,0:T(8,128)(2,1)S(1)} %get-tuple-element.192), channel_id=1, source_target_pairs={{0,4},{4,8},{8,12},{12,16},{16,20},{20,24},{24,28},{28,0},{1,5},{5... | collective-permute-start | bytes 786440 | tf_op jit(solution)/shard_map/ppermute | solution.py:30
  32.9 13.7 %collective-permute-start.1 = (bf16[1024,128]{1,0:T(8,128)(2,1)S(1)}, bf16[1024,128]{1,0:T(8,128)(2,1)S(1)}, u32[]{:S(2)}, u32[]{:S(2)}) collective-permute-start(bf16[1024,128]{1,0:T(8,128)(2,1)S(1)} %get-tuple-element.192), channel_id=1, source_target_pairs={{0,28},{4,0},{8,4},{12,8},{16,12},{20,16},{24,20},{28,24},{1,29},{... | collective-permute-start | bytes 786440 | tf_op jit(solution)/shard_map/ppermute | solution.py:36
  44.0 12.9 %collective-permute-start.2 = (bf16[1024,128]{1,0:T(8,128)(2,1)S(1)}, bf16[1024,128]{1,0:T(8,128)(2,1)S(1)}, u32[]{:S(2)}, u32[]{:S(2)}) collective-permute-start(bf16[1024,128]{1,0:T(8,128)(2,1)S(1)} %collective-permute-done), channel_id=1, source_target_pairs={{0,4},{4,8},{8,12},{12,16},{16,20},{20,24},{24,28},{28,0},{1,5},{5... | collective-permute-start | bytes 786440 | tf_op jit(solution)/shard_map/ppermute | solution.py:30
  46.5 13.1 %collective-permute-start.3 = (bf16[1024,128]{1,0:T(8,128)(2,1)S(1)}, bf16[1024,128]{1,0:T(8,128)(2,1)S(1)}, u32[]{:S(2)}, u32[]{:S(2)}) collective-permute-start(bf16[1024,128]{1,0:T(8,128)(2,1)S(1)} %collective-permute-done.1), channel_id=1, source_target_pairs={{0,28},{4,0},{8,4},{12,8},{16,12},{20,16},{24,20},{28,24},{1,29},{... | collective-permute-start | bytes 786440 | tf_op jit(solution)/shard_map/ppermute | solution.py:36
  56.9 12.2 %collective-permute-start.4 = (bf16[1024,128]{1,0:T(8,128)(2,1)S(1)}, bf16[1024,128]{1,0:T(8,128)(2,1)S(1)}, u32[]{:S(2)}, u32[]{:S(2)}) collective-permute-start(bf16[1024,128]{1,0:T(8,128)(2,1)S(1)} %collective-permute-done.2), channel_id=1, source_target_pairs={{0,4},{4,8},{8,12},{12,16},{16,20},{20,24},{24,28},{28,0},{1,5},{5... | collective-permute-start | bytes 786440 | tf_op jit(solution)/shard_map/ppermute | solution.py:30
  59.6 12.2 %collective-permute-start.5 = (bf16[1024,128]{1,0:T(8,128)(2,1)S(1)}, bf16[1024,128]{1,0:T(8,128)(2,1)S(1)}, u32[]{:S(2)}, u32[]{:S(2)}) collective-permute-start(bf16[1024,128]{1,0:T(8,128)(2,1)S(1)} %collective-permute-done.3), channel_id=1, source_target_pairs={{0,28},{4,0},{8,4},{12,8},{16,12},{20,16},{24,20},{28,24},{1,29},{... | collective-permute-start | bytes 786440 | tf_op jit(solution)/shard_map/ppermute | solution.py:36
  69.2 12.4 %collective-permute-start.6 = (bf16[1024,128]{1,0:T(8,128)(2,1)S(1)}, bf16[1024,128]{1,0:T(8,128)(2,1)S(1)}, u32[]{:S(2)}, u32[]{:S(2)}) collective-permute-start(bf16[1024,128]{1,0:T(8,128)(2,1)S(1)} %collective-permute-done.4), channel_id=1, source_target_pairs={{0,4},{4,8},{8,12},{12,16},{16,20},{20,24},{24,28},{28,0},{1,5},{5... | collective-permute-start | bytes 786440 | tf_op jit(solution)/shard_map/ppermute | solution.py:30
  96.3 5.8 copy-start
  101.3 6.7 %copy-start.11 = (f32[8,256,256]{2,1,0:T(8,128)}, f32[8,256,256]{2,1,0:T(8,128)S(1)}, u32[]{:S(2)}) copy-start(f32[8,256,256]{2,1,0:T(8,128)S(1)} %fusion.29) | copy-start | bytes 6291460 | tf_op jit(solution)/shard_map/while
  157.8 5.7 copy-start
  162.9 6.7 %copy-start.11 = (f32[8,256,256]{2,1,0:T(8,128)}, f32[8,256,256]{2,1,0:T(8,128)S(1)}, u32[]{:S(2)}) copy-start(f32[8,256,256]{2,1,0:T(8,128)S(1)} %fusion.29) | copy-start | bytes 6291460 | tf_op jit(solution)/shard_map/while
  219.7 5.8 copy-start
  224.8 6.7 %copy-start.11 = (f32[8,256,256]{2,1,0:T(8,128)}, f32[8,256,256]{2,1,0:T(8,128)S(1)}, u32[]{:S(2)}) copy-start(f32[8,256,256]{2,1,0:T(8,128)S(1)} %fusion.29) | copy-start | bytes 6291460 | tf_op jit(solution)/shard_map/while
  281.4 5.8 copy-start
  286.4 6.7 %copy-start.11 = (f32[8,256,256]{2,1,0:T(8,128)}, f32[8,256,256]{2,1,0:T(8,128)S(1)}, u32[]{:S(2)}) copy-start(f32[8,256,256]{2,1,0:T(8,128)S(1)} %fusion.29) | copy-start | bytes 6291460 | tf_op jit(solution)/shard_map/while
  334.9 245.9 %reduce-scatter.2.cloned.1.call-start = ((), (), s32[]{:S(2)}) async-start(), calls=%async_computation.3 | async-start | bytes 4718592 | tf_op jit(solution)/shard_map/reduce_scatter | solution.py:133
  334.9 1.0 copy-start.2
  334.9 1.2 copy-start.4
  334.9 1.6 copy-start.9
  334.9 40.7 %copy-start.8 = (f32[1024]{0:T(1024)S(1)}, f32[1024]{0:T(1024)}, u32[]{:S(2)}) copy-start(f32[1024]{0:T(1024)} %param.16) | copy-start | bytes 12292
  335.0 40.7 %copy-start.7 = (f32[2048]{0:T(1024)S(1)}, f32[2048]{0:T(1024)}, u32[]{:S(2)}) copy-start(f32[2048]{0:T(1024)} %param.13) | copy-start | bytes 24580
  494.9 85.9 %copy-start.6 = (bf16[1024,128]{1,0:T(8,128)(2,1)S(1)}, bf16[1024,128]{1,0:T(8,128)(2,1)}, u32[]{:S(2)}) copy-start(bf16[1024,128]{1,0:T(8,128)(2,1)} %copy-done.5) | copy-start | bytes 786436
Sparse Core Ops, SparseCore 0:
  24.9 37.7 all-gather.1
  335.0 153.2 all-reduce.2
  491.9 88.8 reduce-scatter.1
